TPU v7x, 256 devices: a whole 4x4x8 slice. The times are simulated.
256 devices in a mesh: resp: 32 (over y, x, core), head: 8 (over z).
Axes of the slice: x: 4, y: 4, z: 8, core: 2. Of those that a mesh axis runs over, the one named last changes fastest.
Arguments:
- queries: bfloat16 [32, 512, 8192], P('resp', None, 'head'), may hold values from -18 to 18
- key_states: bfloat16 [32, 512, 1024], P('resp', None, 'head'), may hold values from -6 to 6
- value_states: bfloat16 [32, 512, 1024], P('resp', None, 'head'), may hold values from -30 to 30
- partners: int32 [32, 3], P('resp'), may hold values from 0 to 31, as said below
- counts: int32 [32], P('resp'), may hold values from 1 to 3, as said below
- norm_gain: float32 [8192], P('head'), may hold values from 0.25 to 1.75
- out_grad: bfloat16 [32, 512, 8192], P('resp', None, 'head'), may hold values from -6 to 6
Outputs:
- normed_out: bfloat16 [32, 512, 8192], P('resp', None, 'head')
- query_grads: bfloat16 [32, 512, 8192], P('resp', None, 'head')
- key_grads: bfloat16 [32, 512, 1024], P('resp', None, 'head')
- value_grads: bfloat16 [32, 512, 1024], P('resp', None, 'head')
Inputs may be any that keep to these rules, and one draw needn't show every extreme that they name: Row r lists 3 different partners, all in the aligned block of 8 responses that holds r, none equal to r; the first counts[r] of them are live, the rest unused. Live partnership is symmetric: b is a live partner of a exactly when a is a live partner of b. `counts`: some response has 3 live partners.
All inputs are finite; a program needn't handle non-finite values.
Results may differ from a plain program's by a relative error of at most 0.015.
Values may be sent and summed in bfloat16 or wider, within the bound.
No kernel may reach another device: no remote copies, remote signals or barrier semaphores. Data moves between devices by JAX's collectives and lax.ppermute only.
A program may use at most 64 MiB of HBM per device.

v0:
```python
import jax
import jax.numpy as jnp
from jax import lax
from jax.sharding import PartitionSpec as P

HD = 128
D = 8192
GROUP = 8
EPSILON = 1e-05
NEG_FLOOR = -1e30


def add_row(buffer, addend, row_index):
    current = lax.dynamic_index_in_dim(buffer, row_index, 0, keepdims=False)
    return lax.dynamic_update_index_in_dim(buffer, current + addend, row_index, 0)


def body(queries, key_states, value_states, partners, counts, norm_gain, out_grad):
    my_index = lax.axis_index("resp")
    seq_len = queries.shape[1]
    kv_cols = key_states.shape[2]
    kv_heads = kv_cols // HD
    per_group = queries.shape[2] // kv_cols
    resp_count = lax.axis_size("resp")

    def by_distance(block):
        rows = [block]
        for distance in range(1, GROUP):
            route = [(low, low ^ distance) for low in range(resp_count)]
            rows.append(lax.ppermute(block, "resp", route))
        return jnp.concatenate(rows, 0)

    cluster_key_rows = by_distance(key_states)
    group_values = by_distance(value_states)
    query_heads = queries[0].reshape(seq_len, kv_heads, per_group, HD)
    score_scale = HD ** (-0.5)
    mate_rows = jnp.bitwise_xor(partners[0], my_index)
    live_count = counts[0]

    def partner_block_tile(slot_index):
        mate_row = mate_rows[slot_index]
        mate_keys = lax.dynamic_index_in_dim(cluster_key_rows, mate_row, 0, keepdims=False).reshape(
            seq_len, kv_heads, HD
        )
        mate_values = lax.dynamic_index_in_dim(group_values, mate_row, 0, keepdims=False).reshape(
            seq_len, kv_heads, HD
        )
        return (mate_keys, mate_values)

    def score_block(mate_keys):
        return (
            jnp.einsum("qhgd,khd->qhgk", query_heads, mate_keys, preferred_element_type=jnp.float32)
            * score_scale
        )

    def forward_step(slot_index, running):
        running_max, denominator, weighted = running
        mate_keys, mate_values = partner_block_tile(slot_index)
        scores = score_block(mate_keys)
        new_max = jnp.maximum(running_max, jnp.max(scores, -1))
        rescale = jnp.exp(running_max - new_max)
        weights = jnp.exp(scores - new_max[..., None])
        denominator = denominator * rescale + jnp.sum(weights, -1)
        weighted = weighted * rescale[..., None] + jnp.einsum(
            "qhgk,khd->qhgd",
            weights.astype(jnp.bfloat16),
            mate_values,
            preferred_element_type=jnp.float32,
        )
        return (new_max, denominator, weighted)

    stat_shape = (seq_len, kv_heads, per_group)
    start_state = (
        jnp.full(stat_shape, NEG_FLOOR, jnp.float32),
        jnp.zeros(stat_shape, jnp.float32),
        jnp.zeros(stat_shape + (HD,), jnp.float32),
    )
    running_max, denominator, weighted = lax.fori_loop(0, live_count, forward_step, start_state)
    attention = (weighted / denominator[..., None]).astype(jnp.bfloat16)
    log_total = running_max + jnp.log(denominator)
    attention_flat = attention.reshape(seq_len, -1).astype(jnp.float32)
    square_sums = lax.psum(jnp.sum(attention_flat * attention_flat, -1), "head")
    inverse_rms = lax.rsqrt(square_sums / D + EPSILON)
    normed_out = (attention_flat * inverse_rms[:, None] * norm_gain).astype(jnp.bfloat16)[None]
    scaled_grad = out_grad[0].astype(jnp.float32) * norm_gain
    dot_sums = lax.psum(jnp.sum(attention_flat * scaled_grad, -1), "head")
    attention_grad = (
        inverse_rms[:, None] * scaled_grad
        - attention_flat * (inverse_rms**3 * dot_sums / D)[:, None]
    )
    attention_grad = attention_grad.astype(jnp.bfloat16).reshape(seq_len, kv_heads, per_group, HD)
    row_delta = jnp.sum(attention_grad.astype(jnp.float32) * attention.astype(jnp.float32), -1)

    def backward_step(slot_index, running):
        query_grad, key_buffer, value_storage = running
        mate_keys, mate_values = partner_block_tile(slot_index)
        back_probs = jnp.exp(score_block(mate_keys) - log_total[..., None])
        value_term = jnp.einsum(
            "qhgk,qhgd->khd",
            back_probs.astype(jnp.bfloat16),
            attention_grad,
            preferred_element_type=jnp.float32,
        )
        prob_grad = jnp.einsum(
            "qhgd,khd->qhgk", attention_grad, mate_values, preferred_element_type=jnp.float32
        )
        score_grad = (back_probs * (prob_grad - row_delta[..., None])).astype(jnp.bfloat16)
        query_grad = query_grad + score_scale * jnp.einsum(
            "qhgk,khd->qhgd", score_grad, mate_keys, preferred_element_type=jnp.float32
        )
        key_term = score_scale * jnp.einsum(
            "qhgk,qhgd->khd", score_grad, query_heads, preferred_element_type=jnp.float32
        )
        mate_row = mate_rows[slot_index]
        key_buffer = add_row(key_buffer, key_term.reshape(seq_len, kv_cols), mate_row)
        value_storage = add_row(value_storage, value_term.reshape(seq_len, kv_cols), mate_row)
        return (query_grad, key_buffer, value_storage)

    zero_buffer = jnp.zeros((GROUP, seq_len, kv_cols), jnp.float32)
    query_grad, key_buffer, value_storage = lax.fori_loop(
        0,
        live_count,
        backward_step,
        (jnp.zeros(stat_shape + (HD,), jnp.float32), zero_buffer, zero_buffer),
    )
    query_grads = query_grad.reshape(seq_len, -1).astype(jnp.bfloat16)[None]

    def to_owners(buffer):
        total = jnp.zeros(buffer.shape[1:], jnp.float32)
        for distance in range(1, GROUP):
            route = [(low, low ^ distance) for low in range(resp_count)]
            sent = buffer[distance].astype(jnp.bfloat16)
            total = total + lax.ppermute(sent, "resp", route).astype(jnp.float32)
        return total[None]

    key_total = to_owners(key_buffer)
    value_total = to_owners(value_storage)
    return (
        normed_out,
        query_grads,
        key_total.astype(jnp.bfloat16),
        value_total.astype(jnp.bfloat16),
    )


def solution(mesh):
    placed = (
        P("resp", None, "head"),
        P("resp", None, "head"),
        P("resp", None, "head"),
        P("resp", None),
        P("resp"),
        P("head"),
        P("resp", None, "head"),
    )
    return jax.shard_map(
        body,
        mesh=mesh,
        in_specs=placed,
        out_specs=(
            P("resp", None, "head"),
            P("resp", None, "head"),
            P("resp", None, "head"),
            P("resp", None, "head"),
        ),
        check_vma=False,
    )
```

profile of v0, /device:TPU:25, one launch (start us, length us, event | category | flops | bytes accessed | tf_op | source)
XLA Modules:
  0.0 200.0 jit_solution(2755921004239567861)
XLA Ops:
  0.6 2.6 %collective-permute-start.5 = (bf16[1,512,128]{2,1,0:T(8,128)(2,1)}, bf16[1,512,128]{2,1,0:T(8,128)(2,1)S(1)}, u32[]{:S(2)}, u32[]{:S(2)}) collective-permute-start(bf16[1,512,128]{2,1,0:T(8,128)(2,1)} %param.12), channel_id=1, source_target_pairs={{0,48},{8,56},{16,32},{24,40},{32,16},{40,24},{48,0},{56,8},{64,11... | collective-permute-start | bytes 393224 | tf_op jit(solution)/shard_map/ppermute | solution.py:30
  4.6 2.5 %collective-permute-start.3 = (bf16[1,512,128]{2,1,0:T(8,128)(2,1)}, bf16[1,512,128]{2,1,0:T(8,128)(2,1)}, u32[]{:S(2)}, u32[]{:S(2)}) collective-permute-start(bf16[1,512,128]{2,1,0:T(8,128)(2,1)} %param.12), channel_id=1, source_target_pairs={{0,32},{8,40},{16,48},{24,56},{32,0},{40,8},{48,16},{56,24},{64,96... | collective-permute-start | bytes 393224 | tf_op jit(solution)/shard_map/ppermute | solution.py:30
  10.2 2.3 %copy.25 = bf16[1,512,1024]{1,2,0:T(8,128)(2,1)} copy(bf16[1,512,1024]{2,1,0:T(8,128)(2,1)} %param.17) | data formatting | bytes 2097152 | tf_op args[6]
  20.4 2.9 %collective-permute-start.11 = (bf16[1,512,128]{2,1,0:T(8,128)(2,1)S(1)}, bf16[1,512,128]{2,1,0:T(8,128)(2,1)S(1)}, u32[]{:S(2)}, u32[]{:S(2)}) collective-permute-start(bf16[1,512,128]{2,1,0:T(8,128)(2,1)S(1)} %copy-done.10), channel_id=1, source_target_pairs={{0,40},{8,32},{16,56},{24,48},{32,8},{40,0},{48,24},{56,16},{64,10... | collective-permute-start | bytes 393224 | tf_op jit(solution)/shard_map/ppermute | solution.py:30
  29.1 3.9 %collective-permute-done.8 = bf16[1,512,128]{2,1,0:T(8,128)(2,1)S(1)} collective-permute-done((bf16[1,512,128]{2,1,0:T(8,128)(2,1)S(1)}, bf16[1,512,128]{2,1,0:T(8,128)(2,1)S(1)}, u32[]{:S(2)}, u32[]{:S(2)}) %collective-permute-start.8) | collective-permute-done | bytes 131104 | tf_op jit(solution)/shard_map/ppermute | solution.py:30
  33.0 2.3 %collective-permute-start.13 = (bf16[1,512,128]{2,1,0:T(8,128)(2,1)S(1)}, bf16[1,512,128]{2,1,0:T(8,128)(2,1)S(1)}, u32[]{:S(2)}, u32[]{:S(2)}) collective-permute-start(bf16[1,512,128]{2,1,0:T(8,128)(2,1)S(1)} %copy-done.10), channel_id=1, source_target_pairs={{0,56},{8,48},{16,40},{24,32},{32,24},{40,16},{48,8},{56,0},{64,12... | collective-permute-start | bytes 393224 | tf_op jit(solution)/shard_map/ppermute | solution.py:30
  40.7 10.9 %while.28 = (s32[]{:T(128)}, f32[512,1,8]{0,2,1:T(8,128)S(1)}, f32[512,1,8]{0,2,1:T(8,128)S(1)}, f32[512,1,8,128]{0,3,2,1:T(8,128)S(1)}, s32[]{:T(128)}, /*index...) while((s32[]{:T(128)}, f32[512,1,8]{0,2,1:T(8,128)S(1)}, ...), condition=%wide.region_3.4_spmd, body=%wide.region_0.3_spmd.sunk | while | flops 1091579904 | bytes 30933212 | solution.py:78
  44.3 2.2 %bitcast_reduce_fusion.2 = (f32[512,8]{0,1:T(8,128)S(1)}, f32[512,512,8]{1,0,2:T(8,128)S(1)}) fusion(bf16[512,1,8,128]{3,0,2,1:T(8,128)(2,1)S(1)} %get-tuple-element.393, bf16[8,512,128]{2,1,0:T(8,128)(2,1)} %get-tuple-element.392, s32[]{:T(128)S(6)} %select_n.27), kind=kOutput, calls=%fused_computation.1.clone.1 | convolution fusion | flops 541061120 | bytes 9584644 | tf_op jit(solution)/shard_map/while/body/qhgd,khd->qhgk/dot_general | solution.py:52
  47.9 3.0 %bitcast_add_fusion.7 = f32[512,1,8,128]{0,3,2,1:T(8,128)S(1)} fusion(f32[512,1,8,128]{0,3,2,1:T(8,128)S(1)} %get-tuple-element.376, f32[512,512,8]{1,0,2:T(8,128)S(1)} %get-tuple-element.346, f32[512,8]{0,1:T(8,128)S(1)} %bitcast.272, f32[512,8]{0,1:T(8,128)S(1)} %get-tuple-element.347, bf16[8,512,128]{2,1,0:T(8,128)(2,1)} %get-tuple-element.394, ...), kind=kOutput, calls=%fused_computation.9.clone.1 | convolution fusion | flops 544210944 | bytes 12746756 | tf_op jit(solution)/shard_map/while/body/qhgk,khd->qhgd/dot_general | solution.py:64
  51.6 2.8 %fusion.60 = (f32[512]{0:T(512)S(1)}, f32[512]{0:T(512)S(1)}, bf16[512,1,8,128]{0,3,2,1:T(8,128)(2,1)}) fusion(bf16[512,1,8,128]{0,3,2,1:T(8,128)(2,1)} %bitcast.273, f32[8,128]{1,0:T(8,128)S(1)} %bitcast.281, f32[512,1,8,128]{0,3,2,1:T(8,128)S(1)} %get-tuple-element.119, f32[512,8]{0,1:T(8,128)S(1)} %bitcast.278), kind=kLoop, calls=%fused_computation.61 | loop fusion | flops 4717568 | bytes 4218880 | tf_op jit(solution)/shard_map/reduce_sum | solution.py:86
  54.4 16.4 %all-reduce = (f32[512]{0:T(512)S(1)}, f32[512]{0:T(512)S(1)}) all-reduce(f32[512]{0:T(512)S(1)} %get-tuple-element.156, f32[512]{0:T(512)S(1)} %get-tuple-element.155), channel_id=1, replica_groups=mesh['resp'=32,'head'=8] {'head'}, use_global_device_ids=true, to_apply=%region_5.6 | all-reduce | flops 1024 | bytes 8192 | tf_op jit(solution)/shard_map/psum | solution.py:82
  82.0 19.0 %while.29 = (s32[]{:T(128)}, f32[512,1,8,128]{0,3,2,1:T(8,128)}, f32[8,512,128]{2,1,0:T(8,128)}, f32[8,512,128]{2,1,0:T(8,128)}, s32[]{:T(128)}, /*index=5*/s32[...) while((s32[]{:T(128)}, f32[512,1,8,128]{0,3,2,1:T(8,128)}, ...), condition=%wide.region_10.11_spmd, body=%wide.region_9.10_spmd.sunk | while | flops 2702376960 | bytes 64405816 | solution.py:120
  85.4 2.2 %fusion.101 = f32[512,512,8]{1,0,2:T(8,128)S(1)} fusion(bf16[512,1,8,128]{3,0,2,1:T(8,128)(2,1)S(1)} %get-tuple-element.438, bf16[8,512,128]{2,1,0:T(8,128)(2,1)} %get-tuple-element.437, s32[]{:T(128)S(6)} %select_n.29), kind=kOutput, calls=%fused_computation.44.clone.1 | convolution fusion | flops 536870912 | bytes 9568260 | tf_op jit(solution)/shard_map/while/body/qhgd,khd->qhgk/dot_general | solution.py:52
  87.6 3.3 %fusion.104 = f32[8,512,128]{2,1,0:T(8,128)} fusion(f32[8,512,128]{2,1,0:T(8,128)} %get-tuple-element.418, s32[]{:T(128)S(6)} %select_n.29, f32[512,512,8]{1,0,2:T(8,128)S(1)} %fusion.101, f32[512,8]{0,1:T(8,128)S(1)} %bitcast.274, bf16[512,1,8,128]{3,0,2,1:T(8,128)(2,1)S(1)} %get-tuple-element.441), kind=kOutput, calls=%fused_computation.38.clone.1 | convolution fusion | flops 543227904 | bytes 9977860 | tf_op jit(solution)/shard_map/while/body/qhgk,qhgd->khd/dot_general | solution.py:98
  90.9 3.1 %fusion.102 = bf16[512,8,512]{0,2,1:T(8,128)(2,1)S(1)} fusion(f32[512,512,8]{1,0,2:T(8,128)S(1)} %fusion.101, f32[512,8]{0,1:T(8,128)S(1)} %bitcast.280, f32[512,8]{0,1:T(8,128)S(1)} %bitcast.275, bf16[512,1,8,128]{3,0,2,1:T(8,128)(2,1)S(1)} %get-tuple-element.441, bf16[8,512,128]{2,1,0:T(8,128)(2,1)} %get-tuple-element.440, s32[]{:T(128)S(6)} %select_n.29), kind=kOutput, calls=%fused_computation.30.clone.1 | convolution fusion | flops 547356672 | bytes 13795332 | tf_op jit(solution)/shard_map/while/body/qhgd,khd->qhgk/dot_general | solution.py:104
  94.0 3.1 %fusion.103 = f32[8,512,128]{2,1,0:T(8,128)} fusion(f32[8,512,128]{2,1,0:T(8,128)} %get-tuple-element.417, s32[]{:T(128)S(6)} %select_n.29, bf16[512,8,512]{0,2,1:T(8,128)(2,1)S(1)} %fusion.102, bf16[512,1,8,128]{3,0,2,1:T(8,128)(2,1)S(1)} %get-tuple-element.438), kind=kOutput, calls=%fused_computation.40.clone.1 | convolution fusion | flops 537001984 | bytes 5767172 | tf_op jit(solution)/shard_map/while/body/qhgk,qhgd->khd/dot_general | solution.py:111
  103.0 32.4 %collective-permute-start.21 = (bf16[512,128]{1,0:T(8,128)(2,1)S(1)}, bf16[512,128]{1,0:T(8,128)(2,1)S(1)}, u32[]{:S(2)}, u32[]{:S(2)}) collective-permute-start(bf16[512,128]{1,0:T(8,128)(2,1)S(1)} %get-tuple-element.206), channel_id=1, source_target_pairs={{0,8},{8,0},{16,24},{24,16},{32,40},{40,32},{48,56},{56,48},{64,72... | collective-permute-start | bytes 393224 | tf_op jit(solution)/shard_map/ppermute | solution.py:133
  135.4 29.5 %collective-permute-start.27 = (bf16[512,128]{1,0:T(8,128)(2,1)S(1)}, bf16[512,128]{1,0:T(8,128)(2,1)S(1)}, u32[]{:S(2)}, u32[]{:S(2)}) collective-permute-start(bf16[512,128]{1,0:T(8,128)(2,1)S(1)} %get-tuple-element.207), channel_id=1, source_target_pairs={{0,56},{8,48},{16,40},{24,32},{32,24},{40,16},{48,8},{56,0},{64,12... | collective-permute-start | bytes 393224 | tf_op jit(solution)/shard_map/ppermute | solution.py:133
  165.0 3.3 %collective-permute-start.24 = (bf16[512,128]{1,0:T(8,128)(2,1)S(1)}, bf16[512,128]{1,0:T(8,128)(2,1)S(1)}, u32[]{:S(2)}, u32[]{:S(2)}) collective-permute-start(bf16[512,128]{1,0:T(8,128)(2,1)S(1)} %get-tuple-element.210), channel_id=1, source_target_pairs={{0,32},{8,40},{16,48},{24,56},{32,0},{40,8},{48,16},{56,24},{64,96... | collective-permute-start | bytes 393224 | tf_op jit(solution)/shard_map/ppermute | solution.py:133
  170.3 6.5 %collective-permute-done.26 = bf16[512,128]{1,0:T(8,128)(2,1)S(1)} collective-permute-done((bf16[512,128]{1,0:T(8,128)(2,1)S(1)}, bf16[512,128]{1,0:T(8,128)(2,1)S(1)}, u32[]{:S(2)}, u32[]{:S(2)}) %collective-permute-start.26) | collective-permute-done | bytes 131104 | tf_op jit(solution)/shard_map/ppermute | solution.py:133
  177.8 2.5 %collective-permute-start.20 = (bf16[512,128]{1,0:T(8,128)(2,1)S(1)}, bf16[512,128]{1,0:T(8,128)(2,1)S(1)}, u32[]{:S(2)}, u32[]{:S(2)}) collective-permute-start(bf16[512,128]{1,0:T(8,128)(2,1)S(1)} %get-tuple-element.214), channel_id=1, source_target_pairs={{0,56},{8,48},{16,40},{24,32},{32,24},{40,16},{48,8},{56,0},{64,12... | collective-permute-start | bytes 393224 | tf_op jit(solution)/shard_map/ppermute | solution.py:133
  183.2 3.5 %collective-permute-start.17 = (bf16[512,128]{1,0:T(8,128)(2,1)S(1)}, bf16[512,128]{1,0:T(8,128)(2,1)S(1)}, u32[]{:S(2)}, u32[]{:S(2)}) collective-permute-start(bf16[512,128]{1,0:T(8,128)(2,1)S(1)} %get-tuple-element.217), channel_id=1, source_target_pairs={{0,32},{8,40},{16,48},{24,56},{32,0},{40,8},{48,16},{56,24},{64,96... | collective-permute-start | bytes 393224 | tf_op jit(solution)/shard_map/ppermute | solution.py:133
  188.9 5.5 %collective-permute-done.19 = bf16[512,128]{1,0:T(8,128)(2,1)S(1)} collective-permute-done((bf16[512,128]{1,0:T(8,128)(2,1)S(1)}, bf16[512,128]{1,0:T(8,128)(2,1)S(1)}, u32[]{:S(2)}, u32[]{:S(2)}) %collective-permute-start.19) | collective-permute-done | bytes 131104 | tf_op jit(solution)/shard_map/ppermute | solution.py:133
  196.4 2.8 %collective-permute-done.15 = bf16[512,128]{1,0:T(8,128)(2,1)S(1)} collective-permute-done((bf16[512,128]{1,0:T(8,128)(2,1)S(1)}, bf16[512,128]{1,0:T(8,128)(2,1)S(1)}, u32[]{:S(2)}, u32[]{:S(2)}) %collective-permute-start.15) | collective-permute-done | bytes 131104 | tf_op jit(solution)/shard_map/ppermute | solution.py:133
  (114 shorter events, 53.7 us)
Async XLA Ops:
  0.6 25.4 %collective-permute-start.5 = (bf16[1,512,128]{2,1,0:T(8,128)(2,1)}, bf16[1,512,128]{2,1,0:T(8,128)(2,1)S(1)}, u32[]{:S(2)}, u32[]{:S(2)}) collective-permute-start(bf16[1,512,128]{2,1,0:T(8,128)(2,1)} %param.12), channel_id=1, source_target_pairs={{0,48},{8,56},{16,32},{24,40},{32,16},{40,24},{48,0},{56,8},{64,11... | collective-permute-start | bytes 393224 | tf_op jit(solution)/shard_map/ppermute | solution.py:30
  3.2 21.0 %collective-permute-start.4 = (bf16[1,512,128]{2,1,0:T(8,128)(2,1)}, bf16[1,512,128]{2,1,0:T(8,128)(2,1)}, u32[]{:S(2)}, u32[]{:S(2)}) collective-permute-start(bf16[1,512,128]{2,1,0:T(8,128)(2,1)} %param.12), channel_id=1, source_target_pairs={{0,40},{8,32},{16,56},{24,48},{32,8},{40,0},{48,24},{56,16},{64,10... | collective-permute-start | bytes 393224 | tf_op jit(solution)/shard_map/ppermute | solution.py:30
  4.6 15.8 %collective-permute-start.3 = (bf16[1,512,128]{2,1,0:T(8,128)(2,1)}, bf16[1,512,128]{2,1,0:T(8,128)(2,1)}, u32[]{:S(2)}, u32[]{:S(2)}) collective-permute-start(bf16[1,512,128]{2,1,0:T(8,128)(2,1)} %param.12), channel_id=1, source_target_pairs={{0,32},{8,40},{16,48},{24,56},{32,0},{40,8},{48,16},{56,24},{64,96... | collective-permute-start | bytes 393224 | tf_op jit(solution)/shard_map/ppermute | solution.py:30
  7.0 9.5 %collective-permute-start.1 = (bf16[1,512,128]{2,1,0:T(8,128)(2,1)}, bf16[1,512,128]{2,1,0:T(8,128)(2,1)}, u32[]{:S(2)}, u32[]{:S(2)}) collective-permute-start(bf16[1,512,128]{2,1,0:T(8,128)(2,1)} %param.12), channel_id=1, source_target_pairs={{0,16},{8,24},{16,0},{24,8},{32,48},{40,56},{48,32},{56,40},{64,80... | collective-permute-start | bytes 393224 | tf_op jit(solution)/shard_map/ppermute | solution.py:30
  16.6 9.6 %collective-permute-start.6 = (bf16[1,512,128]{2,1,0:T(8,128)(2,1)S(1)}, bf16[1,512,128]{2,1,0:T(8,128)(2,1)S(1)}, u32[]{:S(2)}, u32[]{:S(2)}) collective-permute-start(bf16[1,512,128]{2,1,0:T(8,128)(2,1)S(1)} %copy-done.9), channel_id=1, source_target_pairs={{0,56},{8,48},{16,40},{24,32},{32,24},{40,16},{48,8},{56,0},{64,12... | collective-permute-start | bytes 393224 | tf_op jit(solution)/shard_map/ppermute | solution.py:30
  19.4 18.6 %collective-permute-start.12 = (bf16[1,512,128]{2,1,0:T(8,128)(2,1)S(1)}, bf16[1,512,128]{2,1,0:T(8,128)(2,1)S(1)}, u32[]{:S(2)}, u32[]{:S(2)}) collective-permute-start(bf16[1,512,128]{2,1,0:T(8,128)(2,1)S(1)} %copy-done.10), channel_id=1, source_target_pairs={{0,48},{8,56},{16,32},{24,40},{32,16},{40,24},{48,0},{56,8},{64,11... | collective-permute-start | bytes 393224 | tf_op jit(solution)/shard_map/ppermute | solution.py:30
  20.4 16.9 %collective-permute-start.11 = (bf16[1,512,128]{2,1,0:T(8,128)(2,1)S(1)}, bf16[1,512,128]{2,1,0:T(8,128)(2,1)S(1)}, u32[]{:S(2)}, u32[]{:S(2)}) collective-permute-start(bf16[1,512,128]{2,1,0:T(8,128)(2,1)S(1)} %copy-done.10), channel_id=1, source_target_pairs={{0,40},{8,32},{16,56},{24,48},{32,8},{40,0},{48,24},{56,16},{64,10... | collective-permute-start | bytes 393224 | tf_op jit(solution)/shard_map/ppermute | solution.py:30
  24.3 12.4 %collective-permute-start.10 = (bf16[1,512,128]{2,1,0:T(8,128)(2,1)S(1)}, bf16[1,512,128]{2,1,0:T(8,128)(2,1)S(1)}, u32[]{:S(2)}, u32[]{:S(2)}) collective-permute-start(bf16[1,512,128]{2,1,0:T(8,128)(2,1)S(1)} %copy-done.10), channel_id=1, source_target_pairs={{0,32},{8,40},{16,48},{24,56},{32,0},{40,8},{48,16},{56,24},{64,96... | collective-permute-start | bytes 393224 | tf_op jit(solution)/shard_map/ppermute | solution.py:30
  26.2 6.8 %collective-permute-start.8 = (bf16[1,512,128]{2,1,0:T(8,128)(2,1)S(1)}, bf16[1,512,128]{2,1,0:T(8,128)(2,1)S(1)}, u32[]{:S(2)}, u32[]{:S(2)}) collective-permute-start(bf16[1,512,128]{2,1,0:T(8,128)(2,1)S(1)} %copy-done.10), channel_id=1, source_target_pairs={{0,16},{8,24},{16,0},{24,8},{32,48},{40,56},{48,32},{56,40},{64,80... | collective-permute-start | bytes 393224 | tf_op jit(solution)/shard_map/ppermute | solution.py:30
  27.4 8.5 %collective-permute-start.9 = (bf16[1,512,128]{2,1,0:T(8,128)(2,1)S(1)}, bf16[1,512,128]{2,1,0:T(8,128)(2,1)S(1)}, u32[]{:S(2)}, u32[]{:S(2)}) collective-permute-start(bf16[1,512,128]{2,1,0:T(8,128)(2,1)S(1)} %copy-done.10), channel_id=1, source_target_pairs={{0,24},{8,16},{16,8},{24,0},{32,56},{40,48},{48,40},{56,32},{64,88... | collective-permute-start | bytes 393224 | tf_op jit(solution)/shard_map/ppermute | solution.py:30
  103.0 65.5 %collective-permute-start.21 = (bf16[512,128]{1,0:T(8,128)(2,1)S(1)}, bf16[512,128]{1,0:T(8,128)(2,1)S(1)}, u32[]{:S(2)}, u32[]{:S(2)}) collective-permute-start(bf16[512,128]{1,0:T(8,128)(2,1)S(1)} %get-tuple-element.206), channel_id=1, source_target_pairs={{0,8},{8,0},{16,24},{24,16},{32,40},{40,32},{48,56},{56,48},{64,72... | collective-permute-start | bytes 393224 | tf_op jit(solution)/shard_map/ppermute | solution.py:133
  135.4 34.0 %collective-permute-start.27 = (bf16[512,128]{1,0:T(8,128)(2,1)S(1)}, bf16[512,128]{1,0:T(8,128)(2,1)S(1)}, u32[]{:S(2)}, u32[]{:S(2)}) collective-permute-start(bf16[512,128]{1,0:T(8,128)(2,1)S(1)} %get-tuple-element.207), channel_id=1, source_target_pairs={{0,56},{8,48},{16,40},{24,32},{32,24},{40,16},{48,8},{56,0},{64,12... | collective-permute-start | bytes 393224 | tf_op jit(solution)/shard_map/ppermute | solution.py:133
  164.9 11.9 %collective-permute-start.26 = (bf16[512,128]{1,0:T(8,128)(2,1)S(1)}, bf16[512,128]{1,0:T(8,128)(2,1)S(1)}, u32[]{:S(2)}, u32[]{:S(2)}) collective-permute-start(bf16[512,128]{1,0:T(8,128)(2,1)S(1)} %get-tuple-element.208), channel_id=1, source_target_pairs={{0,48},{8,56},{16,32},{24,40},{32,16},{40,24},{48,0},{56,8},{64,11... | collective-permute-start | bytes 393224 | tf_op jit(solution)/shard_map/ppermute | solution.py:133
  165.0 12.8 %collective-permute-start.25 = (bf16[512,128]{1,0:T(8,128)(2,1)S(1)}, bf16[512,128]{1,0:T(8,128)(2,1)S(1)}, u32[]{:S(2)}, u32[]{:S(2)}) collective-permute-start(bf16[512,128]{1,0:T(8,128)(2,1)S(1)} %get-tuple-element.209), channel_id=1, source_target_pairs={{0,40},{8,32},{16,56},{24,48},{32,8},{40,0},{48,24},{56,16},{64,10... | collective-permute-start | bytes 393224 | tf_op jit(solution)/shard_map/ppermute | solution.py:133
  165.0 18.1 %collective-permute-start.24 = (bf16[512,128]{1,0:T(8,128)(2,1)S(1)}, bf16[512,128]{1,0:T(8,128)(2,1)S(1)}, u32[]{:S(2)}, u32[]{:S(2)}) collective-permute-start(bf16[512,128]{1,0:T(8,128)(2,1)S(1)} %get-tuple-element.210), channel_id=1, source_target_pairs={{0,32},{8,40},{16,48},{24,56},{32,0},{40,8},{48,16},{56,24},{64,96... | collective-permute-start | bytes 393224 | tf_op jit(solution)/shard_map/ppermute | solution.py:133
  168.5 14.6 %collective-permute-start.23 = (bf16[512,128]{1,0:T(8,128)(2,1)S(1)}, bf16[512,128]{1,0:T(8,128)(2,1)S(1)}, u32[]{:S(2)}, u32[]{:S(2)}) collective-permute-start(bf16[512,128]{1,0:T(8,128)(2,1)S(1)} %get-tuple-element.211), channel_id=1, source_target_pairs={{0,24},{8,16},{16,8},{24,0},{32,56},{40,48},{48,40},{56,32},{64,88... | collective-permute-start | bytes 393224 | tf_op jit(solution)/shard_map/ppermute | solution.py:133
  169.4 13.7 %collective-permute-start.22 = (bf16[512,128]{1,0:T(8,128)(2,1)S(1)}, bf16[512,128]{1,0:T(8,128)(2,1)S(1)}, u32[]{:S(2)}, u32[]{:S(2)}) collective-permute-start(bf16[512,128]{1,0:T(8,128)(2,1)S(1)} %get-tuple-element.212), channel_id=1, source_target_pairs={{0,16},{8,24},{16,0},{24,8},{32,48},{40,56},{48,32},{56,40},{64,80... | collective-permute-start | bytes 393224 | tf_op jit(solution)/shard_map/ppermute | solution.py:133
  176.8 9.9 %collective-permute-start.14 = (bf16[512,128]{1,0:T(8,128)(2,1)S(1)}, bf16[512,128]{1,0:T(8,128)(2,1)S(1)}, u32[]{:S(2)}, u32[]{:S(2)}) collective-permute-start(bf16[512,128]{1,0:T(8,128)(2,1)S(1)} %get-tuple-element.213), channel_id=1, source_target_pairs={{0,8},{8,0},{16,24},{24,16},{32,40},{40,32},{48,56},{56,48},{64,72... | collective-permute-start | bytes 393224 | tf_op jit(solution)/shard_map/ppermute | solution.py:133
  177.8 9.5 %collective-permute-start.20 = (bf16[512,128]{1,0:T(8,128)(2,1)S(1)}, bf16[512,128]{1,0:T(8,128)(2,1)S(1)}, u32[]{:S(2)}, u32[]{:S(2)}) collective-permute-start(bf16[512,128]{1,0:T(8,128)(2,1)S(1)} %get-tuple-element.214), channel_id=1, source_target_pairs={{0,56},{8,48},{16,40},{24,32},{32,24},{40,16},{48,8},{56,0},{64,12... | collective-permute-start | bytes 393224 | tf_op jit(solution)/shard_map/ppermute | solution.py:133
  183.0 11.4 %collective-permute-start.19 = (bf16[512,128]{1,0:T(8,128)(2,1)S(1)}, bf16[512,128]{1,0:T(8,128)(2,1)S(1)}, u32[]{:S(2)}, u32[]{:S(2)}) collective-permute-start(bf16[512,128]{1,0:T(8,128)(2,1)S(1)} %get-tuple-element.215), channel_id=1, source_target_pairs={{0,48},{8,56},{16,32},{24,40},{32,16},{40,24},{48,0},{56,8},{64,11... | collective-permute-start | bytes 393224 | tf_op jit(solution)/shard_map/ppermute | solution.py:133
  183.2 11.3 %collective-permute-start.18 = (bf16[512,128]{1,0:T(8,128)(2,1)S(1)}, bf16[512,128]{1,0:T(8,128)(2,1)S(1)}, u32[]{:S(2)}, u32[]{:S(2)}) collective-permute-start(bf16[512,128]{1,0:T(8,128)(2,1)S(1)} %get-tuple-element.216), channel_id=1, source_target_pairs={{0,40},{8,32},{16,56},{24,48},{32,8},{40,0},{48,24},{56,16},{64,10... | collective-permute-start | bytes 393224 | tf_op jit(solution)/shard_map/ppermute | solution.py:133
  183.2 11.3 %collective-permute-start.17 = (bf16[512,128]{1,0:T(8,128)(2,1)S(1)}, bf16[512,128]{1,0:T(8,128)(2,1)S(1)}, u32[]{:S(2)}, u32[]{:S(2)}) collective-permute-start(bf16[512,128]{1,0:T(8,128)(2,1)S(1)} %get-tuple-element.217), channel_id=1, source_target_pairs={{0,32},{8,40},{16,48},{24,56},{32,0},{40,8},{48,16},{56,24},{64,96... | collective-permute-start | bytes 393224 | tf_op jit(solution)/shard_map/ppermute | solution.py:133
  186.7 9.7 %collective-permute-start.16 = (bf16[512,128]{1,0:T(8,128)(2,1)S(1)}, bf16[512,128]{1,0:T(8,128)(2,1)S(1)}, u32[]{:S(2)}, u32[]{:S(2)}) collective-permute-start(bf16[512,128]{1,0:T(8,128)(2,1)S(1)} %get-tuple-element.218), channel_id=1, source_target_pairs={{0,24},{8,16},{16,8},{24,0},{32,56},{40,48},{48,40},{56,32},{64,88... | collective-permute-start | bytes 393224 | tf_op jit(solution)/shard_map/ppermute | solution.py:133
  187.4 11.9 %collective-permute-start.15 = (bf16[512,128]{1,0:T(8,128)(2,1)S(1)}, bf16[512,128]{1,0:T(8,128)(2,1)S(1)}, u32[]{:S(2)}, u32[]{:S(2)}) collective-permute-start(bf16[512,128]{1,0:T(8,128)(2,1)S(1)} %get-tuple-element.219), channel_id=1, source_target_pairs={{0,16},{8,24},{16,0},{24,8},{32,48},{40,56},{48,32},{56,40},{64,80... | collective-permute-start | bytes 393224 | tf_op jit(solution)/shard_map/ppermute | solution.py:133
  (16 other events, 182.0 us)
where the time goes:
time: 201 us; the launch traced here: 200 us
  starting transfers between devices  93.6 us (47%)
  local copies, waits for them, and re-layouts  27.5 us (14%)
  waiting for transfers between devices  23.6 us (12%)
  matrix products  18.7 us (9%)
  blocking collectives  16.4 us (8%)
  other arithmetic  12.1 us (6%)
  loops' own time  7.14 us (4%)
    ppermute x14, starting transfers between devices, to_owners(): total = total + lax.ppermute(sent, 'resp', route).astype(jnp.float32)  75.7 us
    ppermute x14, starting transfers between devices, by_distance(): rows.append(lax.ppermute(block, 'resp', route))  17.9 us
    ppermute x14, waiting for transfers between devices, to_owners(): total = total + lax.ppermute(sent, 'resp', route).astype(jnp.float32)  16.8 us
    psum x1, blocking collectives, body(): square_sums = lax.psum(jnp.sum(attention_flat * attention_flat, -1), 'head')  16.4 us
    unnamed x36, local copies, waits for them, and re-layouts  14 us
    ppermute x14, waiting for transfers between devices, by_distance(): rows.append(lax.ppermute(block, 'resp', route))  6.82 us
    dot_general x2, matrix products, score_block(): jnp.einsum('qhgd,khd->qhgk', query_heads, mate_keys, preferred_element_ty...  4.33 us
  transfers between devices with their start and end apart: 28, of which 8 were waited for; matrix products, arithmetic and copies ran while one was open for 9% of the time, Pallas kernels for 0%

commit v1 on v0

--- a/solution.py
+++ b/solution.py
@@ -79,7 +79,9 @@
     attention = (weighted / denominator[..., None]).astype(jnp.bfloat16)
     log_total = running_max + jnp.log(denominator)
     attention_flat = attention.reshape(seq_len, -1).astype(jnp.float32)
-    square_sums = lax.psum(jnp.sum(attention_flat * attention_flat, -1), "head")
+    square_sums = jnp.sum(
+        lax.all_gather(jnp.sum(attention_flat * attention_flat, -1), "head"), axis=0
+    )
     inverse_rms = lax.rsqrt(square_sums / D + EPSILON)
     normed_out = (attention_flat * inverse_rms[:, None] * norm_gain).astype(jnp.bfloat16)[None]
     scaled_grad = out_grad[0].astype(jnp.float32) * norm_gain

time: 201 us -> 222 us (1.10)
  blocking collectives: 16.4 us -> 32.4 us
  starting transfers between devices: 93.6 us -> 98.2 us
    all_gather x0 -> x1, blocking collectives: none -> 16 us  [body(): lax.all_gather(jnp.sum(attention_flat * attention_flat, -1), 'head')]
    ppermute x14, starting transfers between devices: 75.7 us -> 80.3 us  [to_owners(): total = total + lax.ppermute(sent, 'resp', route).astype(jnp.float32)]
  transfers between devices with their start and end apart: 28 -> 28, of which waited for: 8 -> 8; matrix products, arithmetic and copies ran while one was open for 9% -> 8% of each run, Pallas kernels for 0% -> 0%
where the time goes in v1:
time: 222 us; the launch traced here: 221 us
  starting transfers between devices  98.2 us (44%)
  blocking collectives  32.4 us (15%)
  local copies, waits for them, and re-layouts  27.4 us (12%)
  waiting for transfers between devices  23.6 us (11%)
  matrix products  18.7 us (8%)
  other arithmetic  12.2 us (5%)
  loops' own time  7.08 us (3%)
    ppermute x14, starting transfers between devices, to_owners(): total = total + lax.ppermute(sent, 'resp', route).astype(jnp.float32)  80.3 us
    ppermute x14, starting transfers between devices, by_distance(): rows.append(lax.ppermute(block, 'resp', route))  17.9 us
    ppermute x14, waiting for transfers between devices, to_owners(): total = total + lax.ppermute(sent, 'resp', route).astype(jnp.float32)  16.8 us
    psum x1, blocking collectives, body(): dot_sums = lax.psum(jnp.sum(attention_flat * scaled_grad, -1), 'head')  16.4 us
    all_gather x1, blocking collectives, body(): lax.all_gather(jnp.sum(attention_flat * attention_flat, -1), 'head')  16 us
    unnamed x36, local copies, waits for them, and re-layouts  14 us
    ppermute x14, waiting for transfers between devices, by_distance(): rows.append(lax.ppermute(block, 'resp', route))  6.83 us
  transfers between devices with their start and end apart: 28, of which 8 were waited for; matrix products, arithmetic and copies ran while one was open for 8% of the time, Pallas kernels for 0%

profile of v1, /device:TPU:25, one launch (start us, length us, event | category | flops | bytes accessed | tf_op | source)
XLA Modules:
  0.0 220.5 jit_solution(10513865416272695256)
XLA Ops:
  0.6 2.6 %collective-permute-start.5 = (bf16[1,512,128]{2,1,0:T(8,128)(2,1)}, bf16[1,512,128]{2,1,0:T(8,128)(2,1)S(1)}, u32[]{:S(2)}, u32[]{:S(2)}) collective-permute-start(bf16[1,512,128]{2,1,0:T(8,128)(2,1)} %param.12), channel_id=1, source_target_pairs={{0,48},{8,56},{16,32},{24,40},{32,16},{40,24},{48,0},{56,8},{64,11... | collective-permute-start | bytes 393224 | tf_op jit(solution)/shard_map/ppermute | solution.py:30
  4.6 2.5 %collective-permute-start.3 = (bf16[1,512,128]{2,1,0:T(8,128)(2,1)}, bf16[1,512,128]{2,1,0:T(8,128)(2,1)}, u32[]{:S(2)}, u32[]{:S(2)}) collective-permute-start(bf16[1,512,128]{2,1,0:T(8,128)(2,1)} %param.12), channel_id=1, source_target_pairs={{0,32},{8,40},{16,48},{24,56},{32,0},{40,8},{48,16},{56,24},{64,96... | collective-permute-start | bytes 393224 | tf_op jit(solution)/shard_map/ppermute | solution.py:30
  10.2 2.3 %copy.36 = bf16[1,512,1024]{1,2,0:T(8,128)(2,1)} copy(bf16[1,512,1024]{2,1,0:T(8,128)(2,1)} %param.17) | data formatting | bytes 2097152 | tf_op args[6]
  20.4 2.9 %collective-permute-start.11 = (bf16[1,512,128]{2,1,0:T(8,128)(2,1)S(1)}, bf16[1,512,128]{2,1,0:T(8,128)(2,1)S(1)}, u32[]{:S(2)}, u32[]{:S(2)}) collective-permute-start(bf16[1,512,128]{2,1,0:T(8,128)(2,1)S(1)} %copy-done.10), channel_id=1, source_target_pairs={{0,40},{8,32},{16,56},{24,48},{32,8},{40,0},{48,24},{56,16},{64,10... | collective-permute-start | bytes 393224 | tf_op jit(solution)/shard_map/ppermute | solution.py:30
  29.1 3.9 %collective-permute-done.8 = bf16[1,512,128]{2,1,0:T(8,128)(2,1)S(1)} collective-permute-done((bf16[1,512,128]{2,1,0:T(8,128)(2,1)S(1)}, bf16[1,512,128]{2,1,0:T(8,128)(2,1)S(1)}, u32[]{:S(2)}, u32[]{:S(2)}) %collective-permute-start.8) | collective-permute-done | bytes 131104 | tf_op jit(solution)/shard_map/ppermute | solution.py:30
  33.0 2.3 %collective-permute-start.13 = (bf16[1,512,128]{2,1,0:T(8,128)(2,1)S(1)}, bf16[1,512,128]{2,1,0:T(8,128)(2,1)S(1)}, u32[]{:S(2)}, u32[]{:S(2)}) collective-permute-start(bf16[1,512,128]{2,1,0:T(8,128)(2,1)S(1)} %copy-done.10), channel_id=1, source_target_pairs={{0,56},{8,48},{16,40},{24,32},{32,24},{40,16},{48,8},{56,0},{64,12... | collective-permute-start | bytes 393224 | tf_op jit(solution)/shard_map/ppermute | solution.py:30
  40.7 10.8 %while.28 = (s32[]{:T(128)}, f32[512,1,8]{0,2,1:T(8,128)S(1)}, f32[512,1,8]{0,2,1:T(8,128)S(1)}, f32[512,1,8,128]{0,3,2,1:T(8,128)S(1)}, s32[]{:T(128)}, /*index...) while((s32[]{:T(128)}, f32[512,1,8]{0,2,1:T(8,128)S(1)}, ...), condition=%wide.region_3.4_spmd, body=%wide.region_0.3_spmd.sunk | while | flops 1091579904 | bytes 30933212 | solution.py:78
  44.3 2.2 bitcast_reduce_fusion.2
  47.8 3.0 %bitcast_add_fusion.7 = f32[512,1,8,128]{0,3,2,1:T(8,128)S(1)} fusion(f32[512,1,8,128]{0,3,2,1:T(8,128)S(1)} %get-tuple-element.395, f32[512,512,8]{1,0,2:T(8,128)S(1)} %get-tuple-element.365, f32[512,8]{0,1:T(8,128)S(1)} %bitcast.273, f32[512,8]{0,1:T(8,128)S(1)} %get-tuple-element.366, bf16[8,512,128]{2,1,0:T(8,128)(2,1)} %get-tuple-element.413, ...), kind=kOutput, calls=%fused_computation.9.clone.1 | convolution fusion | flops 544210944 | bytes 12746756 | tf_op jit(solution)/shard_map/while/body/qhgk,khd->qhgd/dot_general | solution.py:64
  51.6 2.8 %fusion.60 = (f32[512]{0:T(512)S(1)}, f32[512]{0:T(512)S(1)}, bf16[512,1,8,128]{0,3,2,1:T(8,128)(2,1)}) fusion(bf16[512,1,8,128]{0,3,2,1:T(8,128)(2,1)} %bitcast.274, f32[8,128]{1,0:T(8,128)S(1)} %bitcast.282, f32[512,1,8,128]{0,3,2,1:T(8,128)S(1)} %get-tuple-element.119, f32[512,8]{0,1:T(8,128)S(1)} %bitcast.279), kind=kLoop, calls=%fused_computation.61 | loop fusion | flops 4717568 | bytes 4218880 | tf_op jit(solution)/shard_map/reduce_sum | solution.py:88
  54.3 16.4 %psum.7 = f32[512]{0:T(512)S(1)} all-reduce(f32[512]{0:T(512)S(1)} %get-tuple-element.176), channel_id=1, replica_groups=mesh['resp'=32,'head'=8] {'head'}, use_global_device_ids=true, to_apply=%region_7.8 | all-reduce | flops 512 | bytes 4096 | tf_op jit(solution)/shard_map/psum | solution.py:88
  70.7 16.0 %all-gather.1 = f32[8,1,512]{2,1,0:T(1,128)S(1)} all-gather(f32[1,1,512]{2,1,0:T(1,128)S(1)} %bitcast.284), channel_id=2, replica_groups=mesh['resp'=32,'head'=8] {'head'}, dimensions={0}, use_global_device_ids=true | all-gather | bytes 18432 | tf_op jit(solution)/shard_map/all_gather | solution.py:83
  98.0 19.0 %while.29 = (s32[]{:T(128)}, f32[512,1,8,128]{0,3,2,1:T(8,128)}, f32[8,512,128]{2,1,0:T(8,128)}, f32[8,512,128]{2,1,0:T(8,128)}, s32[]{:T(128)}, /*index=5*/s32[...) while((s32[]{:T(128)}, f32[512,1,8,128]{0,3,2,1:T(8,128)}, ...), condition=%wide.region_10.11_spmd, body=%wide.region_9.10_spmd.sunk | while | flops 2702376960 | bytes 64405816 | solution.py:122
  103.6 3.3 %fusion.104 = f32[8,512,128]{2,1,0:T(8,128)} fusion(f32[8,512,128]{2,1,0:T(8,128)} %get-tuple-element.437, s32[]{:T(128)S(6)} %select_n.29, f32[512,512,8]{1,0,2:T(8,128)S(1)} %fusion.101, f32[512,8]{0,1:T(8,128)S(1)} %bitcast.275, bf16[512,1,8,128]{3,0,2,1:T(8,128)(2,1)S(1)} %get-tuple-element.460), kind=kOutput, calls=%fused_computation.38.clone.1 | convolution fusion | flops 543227904 | bytes 9977860 | tf_op jit(solution)/shard_map/while/body/qhgk,qhgd->khd/dot_general | solution.py:100
  106.9 3.1 %fusion.102 = bf16[512,8,512]{0,2,1:T(8,128)(2,1)S(1)} fusion(f32[512,512,8]{1,0,2:T(8,128)S(1)} %fusion.101, f32[512,8]{0,1:T(8,128)S(1)} %bitcast.281, f32[512,8]{0,1:T(8,128)S(1)} %bitcast.276, bf16[512,1,8,128]{3,0,2,1:T(8,128)(2,1)S(1)} %get-tuple-element.460, bf16[8,512,128]{2,1,0:T(8,128)(2,1)} %get-tuple-element.459, s32[]{:T(128)S(6)} %select_n.29), kind=kOutput, calls=%fused_computation.30.clone.1 | convolution fusion | flops 547356672 | bytes 13795332 | tf_op jit(solution)/shard_map/while/body/qhgd,khd->qhgk/dot_general | solution.py:106
  110.0 3.0 %fusion.103 = f32[8,512,128]{2,1,0:T(8,128)} fusion(f32[8,512,128]{2,1,0:T(8,128)} %get-tuple-element.436, s32[]{:T(128)S(6)} %select_n.29, bf16[512,8,512]{0,2,1:T(8,128)(2,1)S(1)} %fusion.102, bf16[512,1,8,128]{3,0,2,1:T(8,128)(2,1)S(1)} %get-tuple-element.457), kind=kOutput, calls=%fused_computation.40.clone.1 | convolution fusion | flops 537001984 | bytes 5767172 | tf_op jit(solution)/shard_map/while/body/qhgk,qhgd->khd/dot_general | solution.py:113
  119.0 37.1 %collective-permute-start.21 = (bf16[512,128]{1,0:T(8,128)(2,1)S(1)}, bf16[512,128]{1,0:T(8,128)(2,1)S(1)}, u32[]{:S(2)}, u32[]{:S(2)}) collective-permute-start(bf16[512,128]{1,0:T(8,128)(2,1)S(1)} %get-tuple-element.225), channel_id=1, source_target_pairs={{0,8},{8,0},{16,24},{24,16},{32,40},{40,32},{48,56},{56,48},{64,72... | collective-permute-start | bytes 393224 | tf_op jit(solution)/shard_map/ppermute | solution.py:135
  156.0 29.4 %collective-permute-start.27 = (bf16[512,128]{1,0:T(8,128)(2,1)S(1)}, bf16[512,128]{1,0:T(8,128)(2,1)S(1)}, u32[]{:S(2)}, u32[]{:S(2)}) collective-permute-start(bf16[512,128]{1,0:T(8,128)(2,1)S(1)} %get-tuple-element.226), channel_id=1, source_target_pairs={{0,56},{8,48},{16,40},{24,32},{32,24},{40,16},{48,8},{56,0},{64,12... | collective-permute-start | bytes 393224 | tf_op jit(solution)/shard_map/ppermute | solution.py:135
  185.5 3.3 %collective-permute-start.24 = (bf16[512,128]{1,0:T(8,128)(2,1)S(1)}, bf16[512,128]{1,0:T(8,128)(2,1)S(1)}, u32[]{:S(2)}, u32[]{:S(2)}) collective-permute-start(bf16[512,128]{1,0:T(8,128)(2,1)S(1)} %get-tuple-element.229), channel_id=1, source_target_pairs={{0,32},{8,40},{16,48},{24,56},{32,0},{40,8},{48,16},{56,24},{64,96... | collective-permute-start | bytes 393224 | tf_op jit(solution)/shard_map/ppermute | solution.py:135
  190.8 6.5 %collective-permute-done.26 = bf16[512,128]{1,0:T(8,128)(2,1)S(1)} collective-permute-done((bf16[512,128]{1,0:T(8,128)(2,1)S(1)}, bf16[512,128]{1,0:T(8,128)(2,1)S(1)}, u32[]{:S(2)}, u32[]{:S(2)}) %collective-permute-start.26) | collective-permute-done | bytes 131104 | tf_op jit(solution)/shard_map/ppermute | solution.py:135
  198.3 2.5 %collective-permute-start.20 = (bf16[512,128]{1,0:T(8,128)(2,1)S(1)}, bf16[512,128]{1,0:T(8,128)(2,1)S(1)}, u32[]{:S(2)}, u32[]{:S(2)}) collective-permute-start(bf16[512,128]{1,0:T(8,128)(2,1)S(1)} %get-tuple-element.233), channel_id=1, source_target_pairs={{0,56},{8,48},{16,40},{24,32},{32,24},{40,16},{48,8},{56,0},{64,12... | collective-permute-start | bytes 393224 | tf_op jit(solution)/shard_map/ppermute | solution.py:135
  203.7 3.5 %collective-permute-start.17 = (bf16[512,128]{1,0:T(8,128)(2,1)S(1)}, bf16[512,128]{1,0:T(8,128)(2,1)S(1)}, u32[]{:S(2)}, u32[]{:S(2)}) collective-permute-start(bf16[512,128]{1,0:T(8,128)(2,1)S(1)} %get-tuple-element.236), channel_id=1, source_target_pairs={{0,32},{8,40},{16,48},{24,56},{32,0},{40,8},{48,16},{56,24},{64,96... | collective-permute-start | bytes 393224 | tf_op jit(solution)/shard_map/ppermute | solution.py:135
  209.5 5.5 %collective-permute-done.19 = bf16[512,128]{1,0:T(8,128)(2,1)S(1)} collective-permute-done((bf16[512,128]{1,0:T(8,128)(2,1)S(1)}, bf16[512,128]{1,0:T(8,128)(2,1)S(1)}, u32[]{:S(2)}, u32[]{:S(2)}) %collective-permute-start.19) | collective-permute-done | bytes 131104 | tf_op jit(solution)/shard_map/ppermute | solution.py:135
  217.0 2.8 %collective-permute-done.15 = bf16[512,128]{1,0:T(8,128)(2,1)S(1)} collective-permute-done((bf16[512,128]{1,0:T(8,128)(2,1)S(1)}, bf16[512,128]{1,0:T(8,128)(2,1)S(1)}, u32[]{:S(2)}, u32[]{:S(2)}) %collective-permute-start.15) | collective-permute-done | bytes 131104 | tf_op jit(solution)/shard_map/ppermute | solution.py:135
  (116 shorter events, 55.8 us)
Async XLA Ops:
  0.6 25.4 %collective-permute-start.5 = (bf16[1,512,128]{2,1,0:T(8,128)(2,1)}, bf16[1,512,128]{2,1,0:T(8,128)(2,1)S(1)}, u32[]{:S(2)}, u32[]{:S(2)}) collective-permute-start(bf16[1,512,128]{2,1,0:T(8,128)(2,1)} %param.12), channel_id=1, source_target_pairs={{0,48},{8,56},{16,32},{24,40},{32,16},{40,24},{48,0},{56,8},{64,11... | collective-permute-start | bytes 393224 | tf_op jit(solution)/shard_map/ppermute | solution.py:30
  3.2 21.0 %collective-permute-start.4 = (bf16[1,512,128]{2,1,0:T(8,128)(2,1)}, bf16[1,512,128]{2,1,0:T(8,128)(2,1)}, u32[]{:S(2)}, u32[]{:S(2)}) collective-permute-start(bf16[1,512,128]{2,1,0:T(8,128)(2,1)} %param.12), channel_id=1, source_target_pairs={{0,40},{8,32},{16,56},{24,48},{32,8},{40,0},{48,24},{56,16},{64,10... | collective-permute-start | bytes 393224 | tf_op jit(solution)/shard_map/ppermute | solution.py:30
  4.6 15.8 %collective-permute-start.3 = (bf16[1,512,128]{2,1,0:T(8,128)(2,1)}, bf16[1,512,128]{2,1,0:T(8,128)(2,1)}, u32[]{:S(2)}, u32[]{:S(2)}) collective-permute-start(bf16[1,512,128]{2,1,0:T(8,128)(2,1)} %param.12), channel_id=1, source_target_pairs={{0,32},{8,40},{16,48},{24,56},{32,0},{40,8},{48,16},{56,24},{64,96... | collective-permute-start | bytes 393224 | tf_op jit(solution)/shard_map/ppermute | solution.py:30
  7.0 9.5 %collective-permute-start.1 = (bf16[1,512,128]{2,1,0:T(8,128)(2,1)}, bf16[1,512,128]{2,1,0:T(8,128)(2,1)}, u32[]{:S(2)}, u32[]{:S(2)}) collective-permute-start(bf16[1,512,128]{2,1,0:T(8,128)(2,1)} %param.12), channel_id=1, source_target_pairs={{0,16},{8,24},{16,0},{24,8},{32,48},{40,56},{48,32},{56,40},{64,80... | collective-permute-start | bytes 393224 | tf_op jit(solution)/shard_map/ppermute | solution.py:30
  16.6 9.6 %collective-permute-start.6 = (bf16[1,512,128]{2,1,0:T(8,128)(2,1)S(1)}, bf16[1,512,128]{2,1,0:T(8,128)(2,1)S(1)}, u32[]{:S(2)}, u32[]{:S(2)}) collective-permute-start(bf16[1,512,128]{2,1,0:T(8,128)(2,1)S(1)} %copy-done.9), channel_id=1, source_target_pairs={{0,56},{8,48},{16,40},{24,32},{32,24},{40,16},{48,8},{56,0},{64,12... | collective-permute-start | bytes 393224 | tf_op jit(solution)/shard_map/ppermute | solution.py:30
  19.4 18.6 %collective-permute-start.12 = (bf16[1,512,128]{2,1,0:T(8,128)(2,1)S(1)}, bf16[1,512,128]{2,1,0:T(8,128)(2,1)S(1)}, u32[]{:S(2)}, u32[]{:S(2)}) collective-permute-start(bf16[1,512,128]{2,1,0:T(8,128)(2,1)S(1)} %copy-done.10), channel_id=1, source_target_pairs={{0,48},{8,56},{16,32},{24,40},{32,16},{40,24},{48,0},{56,8},{64,11... | collective-permute-start | bytes 393224 | tf_op jit(solution)/shard_map/ppermute | solution.py:30
  20.4 16.9 %collective-permute-start.11 = (bf16[1,512,128]{2,1,0:T(8,128)(2,1)S(1)}, bf16[1,512,128]{2,1,0:T(8,128)(2,1)S(1)}, u32[]{:S(2)}, u32[]{:S(2)}) collective-permute-start(bf16[1,512,128]{2,1,0:T(8,128)(2,1)S(1)} %copy-done.10), channel_id=1, source_target_pairs={{0,40},{8,32},{16,56},{24,48},{32,8},{40,0},{48,24},{56,16},{64,10... | collective-permute-start | bytes 393224 | tf_op jit(solution)/shard_map/ppermute | solution.py:30
  24.3 12.4 %collective-permute-start.10 = (bf16[1,512,128]{2,1,0:T(8,128)(2,1)S(1)}, bf16[1,512,128]{2,1,0:T(8,128)(2,1)S(1)}, u32[]{:S(2)}, u32[]{:S(2)}) collective-permute-start(bf16[1,512,128]{2,1,0:T(8,128)(2,1)S(1)} %copy-done.10), channel_id=1, source_target_pairs={{0,32},{8,40},{16,48},{24,56},{32,0},{40,8},{48,16},{56,24},{64,96... | collective-permute-start | bytes 393224 | tf_op jit(solution)/shard_map/ppermute | solution.py:30
  26.2 6.8 %collective-permute-start.8 = (bf16[1,512,128]{2,1,0:T(8,128)(2,1)S(1)}, bf16[1,512,128]{2,1,0:T(8,128)(2,1)S(1)}, u32[]{:S(2)}, u32[]{:S(2)}) collective-permute-start(bf16[1,512,128]{2,1,0:T(8,128)(2,1)S(1)} %copy-done.10), channel_id=1, source_target_pairs={{0,16},{8,24},{16,0},{24,8},{32,48},{40,56},{48,32},{56,40},{64,80... | collective-permute-start | bytes 393224 | tf_op jit(solution)/shard_map/ppermute | solution.py:30
  27.4 8.5 %collective-permute-start.9 = (bf16[1,512,128]{2,1,0:T(8,128)(2,1)S(1)}, bf16[1,512,128]{2,1,0:T(8,128)(2,1)S(1)}, u32[]{:S(2)}, u32[]{:S(2)}) collective-permute-start(bf16[1,512,128]{2,1,0:T(8,128)(2,1)S(1)} %copy-done.10), channel_id=1, source_target_pairs={{0,24},{8,16},{16,8},{24,0},{32,56},{40,48},{48,40},{56,32},{64,88... | collective-permute-start | bytes 393224 | tf_op jit(solution)/shard_map/ppermute | solution.py:30
  119.0 70.1 %collective-permute-start.21 = (bf16[512,128]{1,0:T(8,128)(2,1)S(1)}, bf16[512,128]{1,0:T(8,128)(2,1)S(1)}, u32[]{:S(2)}, u32[]{:S(2)}) collective-permute-start(bf16[512,128]{1,0:T(8,128)(2,1)S(1)} %get-tuple-element.225), channel_id=1, source_target_pairs={{0,8},{8,0},{16,24},{24,16},{32,40},{40,32},{48,56},{56,48},{64,72... | collective-permute-start | bytes 393224 | tf_op jit(solution)/shard_map/ppermute | solution.py:135
  156.0 33.9 %collective-permute-start.27 = (bf16[512,128]{1,0:T(8,128)(2,1)S(1)}, bf16[512,128]{1,0:T(8,128)(2,1)S(1)}, u32[]{:S(2)}, u32[]{:S(2)}) collective-permute-start(bf16[512,128]{1,0:T(8,128)(2,1)S(1)} %get-tuple-element.226), channel_id=1, source_target_pairs={{0,56},{8,48},{16,40},{24,32},{32,24},{40,16},{48,8},{56,0},{64,12... | collective-permute-start | bytes 393224 | tf_op jit(solution)/shard_map/ppermute | solution.py:135
  185.4 11.9 %collective-permute-start.26 = (bf16[512,128]{1,0:T(8,128)(2,1)S(1)}, bf16[512,128]{1,0:T(8,128)(2,1)S(1)}, u32[]{:S(2)}, u32[]{:S(2)}) collective-permute-start(bf16[512,128]{1,0:T(8,128)(2,1)S(1)} %get-tuple-element.227), channel_id=1, source_target_pairs={{0,48},{8,56},{16,32},{24,40},{32,16},{40,24},{48,0},{56,8},{64,11... | collective-permute-start | bytes 393224 | tf_op jit(solution)/shard_map/ppermute | solution.py:135
  185.5 12.8 %collective-permute-start.25 = (bf16[512,128]{1,0:T(8,128)(2,1)S(1)}, bf16[512,128]{1,0:T(8,128)(2,1)S(1)}, u32[]{:S(2)}, u32[]{:S(2)}) collective-permute-start(bf16[512,128]{1,0:T(8,128)(2,1)S(1)} %get-tuple-element.228), channel_id=1, source_target_pairs={{0,40},{8,32},{16,56},{24,48},{32,8},{40,0},{48,24},{56,16},{64,10... | collective-permute-start | bytes 393224 | tf_op jit(solution)/shard_map/ppermute | solution.py:135
  185.5 18.1 %collective-permute-start.24 = (bf16[512,128]{1,0:T(8,128)(2,1)S(1)}, bf16[512,128]{1,0:T(8,128)(2,1)S(1)}, u32[]{:S(2)}, u32[]{:S(2)}) collective-permute-start(bf16[512,128]{1,0:T(8,128)(2,1)S(1)} %get-tuple-element.229), channel_id=1, source_target_pairs={{0,32},{8,40},{16,48},{24,56},{32,0},{40,8},{48,16},{56,24},{64,96... | collective-permute-start | bytes 393224 | tf_op jit(solution)/shard_map/ppermute | solution.py:135
  189.1 14.6 %collective-permute-start.23 = (bf16[512,128]{1,0:T(8,128)(2,1)S(1)}, bf16[512,128]{1,0:T(8,128)(2,1)S(1)}, u32[]{:S(2)}, u32[]{:S(2)}) collective-permute-start(bf16[512,128]{1,0:T(8,128)(2,1)S(1)} %get-tuple-element.230), channel_id=1, source_target_pairs={{0,24},{8,16},{16,8},{24,0},{32,56},{40,48},{48,40},{56,32},{64,88... | collective-permute-start | bytes 393224 | tf_op jit(solution)/shard_map/ppermute | solution.py:135
  190.0 13.7 %collective-permute-start.22 = (bf16[512,128]{1,0:T(8,128)(2,1)S(1)}, bf16[512,128]{1,0:T(8,128)(2,1)S(1)}, u32[]{:S(2)}, u32[]{:S(2)}) collective-permute-start(bf16[512,128]{1,0:T(8,128)(2,1)S(1)} %get-tuple-element.231), channel_id=1, source_target_pairs={{0,16},{8,24},{16,0},{24,8},{32,48},{40,56},{48,32},{56,40},{64,80... | collective-permute-start | bytes 393224 | tf_op jit(solution)/shard_map/ppermute | solution.py:135
  197.3 9.9 %collective-permute-start.14 = (bf16[512,128]{1,0:T(8,128)(2,1)S(1)}, bf16[512,128]{1,0:T(8,128)(2,1)S(1)}, u32[]{:S(2)}, u32[]{:S(2)}) collective-permute-start(bf16[512,128]{1,0:T(8,128)(2,1)S(1)} %get-tuple-element.232), channel_id=1, source_target_pairs={{0,8},{8,0},{16,24},{24,16},{32,40},{40,32},{48,56},{56,48},{64,72... | collective-permute-start | bytes 393224 | tf_op jit(solution)/shard_map/ppermute | solution.py:135
  198.3 9.5 %collective-permute-start.20 = (bf16[512,128]{1,0:T(8,128)(2,1)S(1)}, bf16[512,128]{1,0:T(8,128)(2,1)S(1)}, u32[]{:S(2)}, u32[]{:S(2)}) collective-permute-start(bf16[512,128]{1,0:T(8,128)(2,1)S(1)} %get-tuple-element.233), channel_id=1, source_target_pairs={{0,56},{8,48},{16,40},{24,32},{32,24},{40,16},{48,8},{56,0},{64,12... | collective-permute-start | bytes 393224 | tf_op jit(solution)/shard_map/ppermute | solution.py:135
  203.6 11.4 %collective-permute-start.19 = (bf16[512,128]{1,0:T(8,128)(2,1)S(1)}, bf16[512,128]{1,0:T(8,128)(2,1)S(1)}, u32[]{:S(2)}, u32[]{:S(2)}) collective-permute-start(bf16[512,128]{1,0:T(8,128)(2,1)S(1)} %get-tuple-element.234), channel_id=1, source_target_pairs={{0,48},{8,56},{16,32},{24,40},{32,16},{40,24},{48,0},{56,8},{64,11... | collective-permute-start | bytes 393224 | tf_op jit(solution)/shard_map/ppermute | solution.py:135
  203.7 11.3 %collective-permute-start.18 = (bf16[512,128]{1,0:T(8,128)(2,1)S(1)}, bf16[512,128]{1,0:T(8,128)(2,1)S(1)}, u32[]{:S(2)}, u32[]{:S(2)}) collective-permute-start(bf16[512,128]{1,0:T(8,128)(2,1)S(1)} %get-tuple-element.235), channel_id=1, source_target_pairs={{0,40},{8,32},{16,56},{24,48},{32,8},{40,0},{48,24},{56,16},{64,10... | collective-permute-start | bytes 393224 | tf_op jit(solution)/shard_map/ppermute | solution.py:135
  203.7 11.3 %collective-permute-start.17 = (bf16[512,128]{1,0:T(8,128)(2,1)S(1)}, bf16[512,128]{1,0:T(8,128)(2,1)S(1)}, u32[]{:S(2)}, u32[]{:S(2)}) collective-permute-start(bf16[512,128]{1,0:T(8,128)(2,1)S(1)} %get-tuple-element.236), channel_id=1, source_target_pairs={{0,32},{8,40},{16,48},{24,56},{32,0},{40,8},{48,16},{56,24},{64,96... | collective-permute-start | bytes 393224 | tf_op jit(solution)/shard_map/ppermute | solution.py:135
  207.2 9.7 %collective-permute-start.16 = (bf16[512,128]{1,0:T(8,128)(2,1)S(1)}, bf16[512,128]{1,0:T(8,128)(2,1)S(1)}, u32[]{:S(2)}, u32[]{:S(2)}) collective-permute-start(bf16[512,128]{1,0:T(8,128)(2,1)S(1)} %get-tuple-element.237), channel_id=1, source_target_pairs={{0,24},{8,16},{16,8},{24,0},{32,56},{40,48},{48,40},{56,32},{64,88... | collective-permute-start | bytes 393224 | tf_op jit(solution)/shard_map/ppermute | solution.py:135
  207.9 11.9 %collective-permute-start.15 = (bf16[512,128]{1,0:T(8,128)(2,1)S(1)}, bf16[512,128]{1,0:T(8,128)(2,1)S(1)}, u32[]{:S(2)}, u32[]{:S(2)}) collective-permute-start(bf16[512,128]{1,0:T(8,128)(2,1)S(1)} %get-tuple-element.238), channel_id=1, source_target_pairs={{0,16},{8,24},{16,0},{24,8},{32,48},{40,56},{48,32},{56,40},{64,80... | collective-permute-start | bytes 393224 | tf_op jit(solution)/shard_map/ppermute | solution.py:135
  (16 other events, 202.6 us)
